TPU v7x, 32 devices: a whole 2x2x4 slice. The times are simulated.
32 devices in a mesh: dom: 8 (over z, x), grp: 4 (over y, core).
Axes of the slice: x: 2, y: 2, z: 4, core: 2. Of those that a mesh axis runs over, the one named last changes fastest.
Arguments:
- x_current: bfloat16 [131072, 128], P(('dom', 'grp')), may hold values from -6 to 6
- x_cached: bfloat16 [131072, 128], P(('dom', 'grp')), may hold values from -6 to 6
- w_self: bfloat16 [128, 512], replicated, may hold values from -0.5 to 0.5
- w_neigh: bfloat16 [128, 512], replicated, may hold values from -1 to 1
- bias: float32 [512], replicated, may hold values from -3 to 3
- tile_columns: int32 [1024, 40], P(('dom', 'grp')), may hold values from 0 to 159
- tile_count: int32 [1024], P(('dom', 'grp')), may hold values from 1 to 40, as said below
- adjacency: int32 [1024, 40, 2048], P(('dom', 'grp')), may hold values from 0 to 255, as said below
- degree: int32 [131072], P(('dom', 'grp')), may hold values from 1 to 5128, as said below
- boundary_blocks: int32 [32, 1], P(('dom', 'grp')), may hold values from 0 to 31
Outputs:
- hidden: bfloat16 [131072, 512], P(('dom', 'grp'))
Inputs may be any that keep to these rules, and one draw needn't show every extreme that they name: `tile_count`: every device has a row block with all 40 slots live. `adjacency`: 8 entries of a tile row packed into each word, bit b for column 8 c + b. `degree`: at least the number of ones in the row of the live tiles of the node's row block.
All inputs are finite; a program needn't handle non-finite values.
Results may differ from a plain program's by a relative error of at most 0.0025.
Values may be sent and summed in bfloat16 or wider, within the bound.
No kernel may reach another device: no remote copies, remote signals or barrier semaphores. Data moves between devices by JAX's collectives and lax.ppermute only.
A program may use at most 192 MiB of HBM per device.

v0:
```python
import functools

import ml_dtypes
import numpy as np

import jax
import jax.numpy as jnp
from jax import lax
from jax.experimental import pallas as pl
from jax.experimental.pallas import tpu as pltpu
from jax.sharding import PartitionSpec as P

CHUNK = 8


def _expand_matrix(tile):
    rows = np.arange(tile)[:, None]
    cols = np.arange(8 * tile)[None, :]
    s = cols // tile
    j = cols % tile
    hit = rows == (tile // 8) * s + j // 8
    scale = (2.0 ** (7 - j % 8)).astype(np.float32)
    return np.where(hit, scale, 0.0).astype(ml_dtypes.bfloat16)


def _perm_matrix(tile):
    kk = tile // 8
    rows = np.arange(tile)[:, None]
    cols = np.arange(tile)[None, :]
    return rows == 8 * (cols % kk) + cols // kk


def _layer_kernel(cols_ref, counts_ref, grp_ref, adj_ref, xc_ref, deg_ref, w_ref, b_ref,
                  mexp_ref, perm_ref, pick_ref, *rest, per_tile, tile, n_table, n_grp, dev_blocks,
                  levels, per_dev):
    pieces = rest[:n_grp + 1]
    out_ref, table_ref, sems, words_ref, acc_ref = rest[n_grp + 1:]
    r = pl.program_id(0)
    count = counts_ref[r]
    g = grp_ref[0]
    me = grp_ref[1]
    part = n_grp * dev_blocks

    @pl.when(r == 0)
    def _():
        copies = []
        for d in range(n_grp):
            copies.append(pltpu.make_async_copy(
                pieces[d], table_ref.at[pl.ds(d * dev_blocks, dev_blocks)], sems.at[d]))
        n_halo = n_table - part
        copies.append(pltpu.make_async_copy(
            pieces[n_grp], table_ref.at[pl.ds(part, n_halo)], sems.at[n_grp]))
        for cp in copies:
            cp.start()
        for cp in copies:
            cp.wait()

    kk = tile // 8
    for k in range(kk):
        words_ref[pl.ds(k * per_tile, per_tile), :] = adj_ref[0, :, pl.ds(k * tile, tile)]
    acc_ref[...] = jnp.zeros_like(acc_ref)

    def chunk(c, masked):
            words = jnp.concatenate(
                [words_ref[pl.ds(c * CHUNK + tl, kk, stride=per_tile), :] for tl in range(CHUNK)],
                axis=0)
            spread = jnp.dot(words.astype(jnp.bfloat16), mexp_ref[...],
                             preferred_element_type=jnp.float32)
            bits = (spread.astype(jnp.int32) & 128).astype(jnp.bfloat16)
            rows = []
            for s in range(8):
                rows.append(jnp.concatenate(
                    [bits[tl * kk:(tl + 1) * kk, s * tile:(s + 1) * tile] for tl in range(CHUNK)],
                    axis=1))
            a_cat = jnp.concatenate(rows, axis=0)
            xs = []
            for tl in range(CHUNK):
                t = c * CHUNK + tl
                col = cols_ref[r, t]
                if n_grp == 4:
                    slot = jnp.bitwise_xor(col // dev_blocks, g)
                else:
                    slot = (g - col // dev_blocks + n_grp) % n_grp
                rel = slot * dev_blocks + col % dev_blocks
                h = jnp.maximum(col - part, 0)
                x = jnp.bitwise_xor(h // per_dev, me)
                pos = jnp.int32(0)
                for bit in range(levels):
                    pos = pos + ((x >> bit) & 1) * (1 << (levels - 1 - bit))
                hrel = part + pos * per_dev + h % per_dev
                col = jnp.clip(jnp.where(col < part, rel, hrel), 0, n_table - 1)
                xt = table_ref[col]
                if masked:
                    xt = jnp.where(t < count, xt, jnp.zeros_like(xt))
                xs.append(xt)
            x_cat = jnp.concatenate(xs, axis=0)
            acc_ref[...] += jnp.dot(a_cat, x_cat, preferred_element_type=jnp.float32)

    for c in range(per_tile // CHUNK):
        pl.when((c + 1) * CHUNK <= count)(functools.partial(chunk, c, False))
        pl.when((c * CHUNK < count) & (count < (c + 1) * CHUNK))(functools.partial(chunk, c, True))

    acc = acc_ref[...]
    totals = acc * (1.0 / 128.0)
    deg_row = deg_ref[pl.ds(r, 1), :].astype(jnp.float32)
    deg_perm = jnp.sum(pick_ref[...] * deg_row, axis=1, keepdims=True)
    avg_perm = (totals / deg_perm).astype(jnp.bfloat16)
    avg = jnp.dot(perm_ref[...], avg_perm, preferred_element_type=jnp.float32).astype(jnp.bfloat16)
    lhs = jnp.concatenate([xc_ref[...], avg], axis=1)
    summed = jnp.dot(lhs, w_ref[...], preferred_element_type=jnp.float32) + b_ref[...]
    out_ref[...] = jnp.maximum(summed, 0.0).astype(out_ref.dtype)


def on_device(
    x_current,
    x_cached,
    w_self,
    w_neigh,
    bias,
    tile_columns,
    tile_count,
    adjacency,
    degree,
    boundary_blocks,
):
    node_rows, width = x_current.shape
    row_blocks, per_tile = tile_columns.shape
    tile_rows = node_rows // row_blocks
    hidden = w_self.shape[1]
    kk = tile_rows // 8
    assert per_tile % CHUNK == 0
    n_grp = lax.psum(1, "grp")
    chosen = x_cached.reshape(row_blocks, tile_rows, width)[boundary_blocks[0]]
    n_dom = lax.psum(1, "dom")
    n_dev = n_dom * n_grp
    levels = n_dev.bit_length() - 1
    assert 1 << levels == n_dev
    me = lax.axis_index("dom") * n_grp + lax.axis_index("grp")
    halo_blocks = chosen
    for lv in range(levels):
        mask = n_dev >> (lv + 1)
        theirs = lax.ppermute(halo_blocks, ("dom", "grp"), [(i, i ^ mask) for i in range(n_dev)])
        halo_blocks = jnp.concatenate([halo_blocks, theirs], axis=0)
    own_blocks = x_current.reshape(row_blocks, tile_rows, width)
    pieces = [own_blocks]
    if n_grp == 4:
        near = lax.ppermute(own_blocks, "grp", [(i, i ^ 1) for i in range(4)])
        far = lax.ppermute(own_blocks, "grp", [(i, i ^ 2) for i in range(4)])
        far_near = lax.ppermute(far, "grp", [(i, i ^ 1) for i in range(4)])
        pieces += [near, far, far_near]
    else:
        for d in range(1, n_grp):
            pieces.append(lax.ppermute(own_blocks, "grp", [(i, (i + d) % n_grp) for i in range(n_grp)]))
    pieces.append(halo_blocks)
    n_table = n_grp * row_blocks + halo_blocks.shape[0]
    grp_idx = jnp.stack([lax.axis_index("grp"), me]).astype(jnp.int32)

    deg = degree.reshape(row_blocks, tile_rows)
    w_cat = jnp.concatenate([w_self, w_neigh], axis=0)
    b2 = bias.reshape(1, hidden)
    mexp = jnp.asarray(_expand_matrix(tile_rows))
    perm_np = _perm_matrix(tile_rows)
    perm = jnp.asarray(perm_np.astype(ml_dtypes.bfloat16))
    pick = jnp.asarray(perm_np.T.astype(np.float32))

    kernel = functools.partial(_layer_kernel, per_tile=per_tile, tile=tile_rows, n_table=n_table,
                               n_grp=n_grp, dev_blocks=row_blocks, levels=levels,
                               per_dev=chosen.shape[0])
    grid_spec = pltpu.PrefetchScalarGridSpec(
        num_scalar_prefetch=3,
        grid=(row_blocks,),
        in_specs=[
            pl.BlockSpec((1, per_tile, tile_rows * kk), lambda r, *_: (r, 0, 0)),
            pl.BlockSpec((tile_rows, width), lambda r, *_: (r, 0)),
            pl.BlockSpec((row_blocks, tile_rows), lambda r, *_: (0, 0)),
            pl.BlockSpec((2 * width, hidden), lambda r, *_: (0, 0)),
            pl.BlockSpec((1, hidden), lambda r, *_: (0, 0)),
            pl.BlockSpec((tile_rows, 8 * tile_rows), lambda r, *_: (0, 0)),
            pl.BlockSpec((tile_rows, tile_rows), lambda r, *_: (0, 0)),
            pl.BlockSpec((tile_rows, tile_rows), lambda r, *_: (0, 0)),
        ] + [pl.BlockSpec(memory_space=pl.ANY)] * (n_grp + 1),
        out_specs=pl.BlockSpec((tile_rows, hidden), lambda r, *_: (r, 0)),
        scratch_shapes=[pltpu.VMEM((n_table, tile_rows, width), jnp.bfloat16),
                        pltpu.SemaphoreType.DMA((n_grp + 1,)),
                        pltpu.VMEM((per_tile * kk, tile_rows), jnp.int32),
                        pltpu.VMEM((tile_rows, width), jnp.float32)],
    )
    return pl.pallas_call(
        kernel,
        grid_spec=grid_spec,
        out_shape=jax.ShapeDtypeStruct((node_rows, hidden), jnp.bfloat16),
        compiler_params=pltpu.CompilerParams(
            dimension_semantics=("arbitrary",), vmem_limit_bytes=48 * 1024 * 1024),
    )(tile_columns, tile_count, grp_idx, adjacency, x_current, deg, w_cat, b2, mexp, perm, pick, *pieces)


def solution(mesh):
    in_specs = (
        P(("dom", "grp"), None),
        P(("dom", "grp"), None),
        P(),
        P(),
        P(),
        P(("dom", "grp"), None),
        P(("dom", "grp")),
        P(("dom", "grp"), None, None),
        P(("dom", "grp")),
        P(("dom", "grp"), None),
    )
    out_specs = P(("dom", "grp"), None)
    return jax.shard_map(
        on_device, mesh=mesh, in_specs=in_specs, out_specs=out_specs, check_vma=False
    )
```

profile of v0, /device:TPU:0, one launch (start us, length us, event | category | flops | bytes accessed | tf_op | source)
XLA Modules:
  0.0 110.0 jit_solution(1505203713257898983)
XLA Ops:
  0.0 3.0 %collective-permute-start.1 = (bf16[32,128,128]{2,1,0:T(8,128)(2,1)}, bf16[32,128,128]{2,1,0:T(8,128)(2,1)S(1)}, u32[]{:S(2)}, u32[]{:S(2)}) collective-permute-start(bf16[32,128,128]{2,1,0:T(8,128)(2,1)} %bitcast.11), channel_id=1, source_target_pairs={{0,2},{1,3},{2,0},{3,1},{4,6},{5,7},{6,4},{7,5},{8,10},{9,11},{10,... | collective-permute-start | bytes 3145736 | tf_op jit(solution)/shard_map/ppermute | solution.py:148
  3.7 1.4 %constant_dynamic-update-slice_fusion.4 = (bf16[16,128,128]{2,1,0:T(8,128)(2,1)}, bf16[1,128,128]{2,1,0:T(8,128)(2,1)S(1)}) fusion(bf16[32,128,128]{2,1,0:T(8,128)(2,1)} %bitcast.16, s32[]{:T(128)} %bitcast.7), kind=kLoop, calls=%fused_computation.8 | loop fusion | bytes 98308
  5.0 2.6 %collective-permute-start.3 = (bf16[1,128,128]{2,1,0:T(8,128)(2,1)S(1)}, bf16[1,128,128]{2,1,0:T(8,128)(2,1)S(1)}, u32[]{:S(2)}, u32[]{:S(2)}) collective-permute-start(bf16[1,128,128]{2,1,0:T(8,128)(2,1)S(1)} %get-tuple-element.17), channel_id=1, source_target_pairs={{0,16},{1,17},{2,18},{3,19},{4,20},{5,21},{6,22},{7,23},{8,24},{9,... | collective-permute-start | bytes 98312 | tf_op jit(solution)/shard_map/ppermute | solution.py:142
  7.6 2.2 %collective-permute-done.3 = bf16[1,128,128]{2,1,0:T(8,128)(2,1)S(1)} collective-permute-done((bf16[1,128,128]{2,1,0:T(8,128)(2,1)S(1)}, bf16[1,128,128]{2,1,0:T(8,128)(2,1)S(1)}, u32[]{:S(2)}, u32[]{:S(2)}) %collective-permute-start.3) | collective-permute-done | bytes 32800 | tf_op jit(solution)/shard_map/ppermute | solution.py:142
  9.9 1.6 %collective-permute-start.4 = (bf16[2,128,128]{2,1,0:T(8,128)(2,1)S(1)}, bf16[2,128,128]{2,1,0:T(8,128)(2,1)S(1)}, u32[]{:S(2)}, u32[]{:S(2)}) collective-permute-start(bf16[2,128,128]{2,1,0:T(8,128)(2,1)S(1)} %pad_maximum_fusion.3), channel_id=1, source_target_pairs={{0,8},{1,9},{2,10},{3,11},{4,12},{5,13},{6,14},{7,15},{8,0},{9,1},... | collective-permute-start | bytes 196616 | tf_op jit(solution)/shard_map/ppermute | solution.py:142
  11.5 2.7 %collective-permute-done.4 = bf16[2,128,128]{2,1,0:T(8,128)(2,1)S(1)} collective-permute-done((bf16[2,128,128]{2,1,0:T(8,128)(2,1)S(1)}, bf16[2,128,128]{2,1,0:T(8,128)(2,1)S(1)}, u32[]{:S(2)}, u32[]{:S(2)}) %collective-permute-start.4) | collective-permute-done | bytes 65568 | tf_op jit(solution)/shard_map/ppermute | solution.py:142
  14.2 1.6 %collective-permute-start.5 = (bf16[4,128,128]{2,1,0:T(8,128)(2,1)S(1)}, bf16[4,128,128]{2,1,0:T(8,128)(2,1)S(1)}, u32[]{:S(2)}, u32[]{:S(2)}) collective-permute-start(bf16[4,128,128]{2,1,0:T(8,128)(2,1)S(1)} %pad_maximum_fusion.2), channel_id=1, source_target_pairs={{0,4},{1,5},{2,6},{3,7},{4,0},{5,1},{6,2},{7,3},{8,12},{9,13},{10,... | collective-permute-start | bytes 393224 | tf_op jit(solution)/shard_map/ppermute | solution.py:142
  15.8 0.0 collective-permute-start
  15.8 3.5 %collective-permute-done.5 = bf16[4,128,128]{2,1,0:T(8,128)(2,1)S(1)} collective-permute-done((bf16[4,128,128]{2,1,0:T(8,128)(2,1)S(1)}, bf16[4,128,128]{2,1,0:T(8,128)(2,1)S(1)}, u32[]{:S(2)}, u32[]{:S(2)}) %collective-permute-start.5) | collective-permute-done | bytes 131104 | tf_op jit(solution)/shard_map/ppermute | solution.py:142
  19.3 0.5 collective-permute-start.6
  19.8 7.4 %collective-permute-done.1.rest_2_ = bf16[32,128,128]{2,1,0:T(8,128)(2,1)S(1)} collective-permute-done((bf16[32,128,128]{2,1,0:T(8,128)(2,1)}, bf16[32,128,128]{2,1,0:T(8,128)(2,1)S(1)}, u32[]{:S(2)}, u32[]{:S(2)}) %collective-permute-start.1) | collective-permute-done | bytes 1048608 | tf_op jit(solution)/shard_map/ppermute | solution.py:148
  27.2 0.0 collective-permute-start.2
  27.2 0.6 constant_dynamic-update-slice_fusion.3
  27.8 0.6 constant_dynamic-update-slice_fusion.2
  28.5 0.7 constant_dynamic-update-slice_fusion.1
  29.2 2.8 %collective-permute-done.6 = bf16[8,128,128]{2,1,0:T(8,128)(2,1)S(1)} collective-permute-done((bf16[8,128,128]{2,1,0:T(8,128)(2,1)S(1)}, bf16[8,128,128]{2,1,0:T(8,128)(2,1)S(1)}, u32[]{:S(2)}, u32[]{:S(2)}) %collective-permute-start.6) | collective-permute-done | bytes 262176 | tf_op jit(solution)/shard_map/ppermute | solution.py:142
  32.0 0.8 constant_dynamic-update-slice_fusion
  32.8 0.0 collective-permute-start.7
  32.8 0.1 pad_add_fusion.grp_ref
  32.9 1.0 pad_maximum_fusion.w_ref
  33.9 1.2 %collective-permute-done.7 = bf16[16,128,128]{2,1,0:T(8,128)(2,1)} collective-permute-done((bf16[16,128,128]{2,1,0:T(8,128)(2,1)}, bf16[16,128,128]{2,1,0:T(8,128)(2,1)}, u32[]{:S(2)}, u32[]{:S(2)}) %collective-permute-start.7) | collective-permute-done | bytes 524320 | tf_op jit(solution)/shard_map/ppermute | solution.py:142
  35.0 1.1 %constant_dynamic-update-slice_fusion.5.rest_4_ = bf16[32,128,128]{2,1,0:T(8,128)(2,1)S(1)} fusion(bf16[32,128,128]{2,1,0:T(8,128)(2,1)S(1)} %get-tuple-element.19, bf16[16,128,128]{2,1,0:T(8,128)(2,1)} %collective-permute-done.7), kind=kLoop, calls=%fused_computation.9 | loop fusion | bytes 1048576 | tf_op jit(solution)/shard_map/concatenate | solution.py:143
  36.2 0.0 collective-permute-done.rest_1_
  36.2 0.0 collective-permute-done.2.rest_3_
  36.2 0.0 copy-start
  36.2 1.2 %copy-done = bf16[4096,128]{1,0:T(8,128)(2,1)S(1)} copy-done((bf16[4096,128]{1,0:T(8,128)(2,1)S(1)}, bf16[4096,128]{1,0:T(8,128)(2,1)}, u32[]{:S(2)}) %copy-start) | copy-done | bytes 1048600
  37.4 0.0 copy-start.1
  37.4 0.9 copy-done.1
  38.4 0.0 copy-start.2
  38.4 0.8 copy-done.2
  39.2 0.0 copy-start.3
  39.2 0.8 copy-done.3
  40.0 0.0 copy-start.4
  40.0 0.7 copy-done.4
  40.7 0.0 copy-start.5
  40.7 0.7 copy-done.5
  41.4 0.0 copy-start.6
  41.4 0.7 copy-done.6
  42.1 0.0 copy-start.7
  42.1 0.7 copy-done.7
  42.7 67.2 %shard_map.127 = bf16[4096,512]{1,0:T(8,128)(2,1)} custom-call(s32[32,40]{1,0:T(8,128)S(1)} %copy-done.4, s32[32]{0:T(128)S(1)} %copy-done.7, s32[2]{0:T(128)S(1)} %pad_add_fusion.grp_ref, s32[32,40,2048]{2,1,0:T(8,128)} %adj_ref.1, bf16[4096,128]{1,0:T(8,128)(2,1)S(1)} %copy-done, s32[32,128]{1,0:T(8,128)S(1)} %bitcast.14, ...), custom_call_target="tpu_custom_call" | custom-call | tf_op jit(solution)/shard_map/pallas_call | solution.py:188
  (4 shorter events, 0.1 us)
Async XLA Ops:
  0.0 27.2 %collective-permute-start.1 = (bf16[32,128,128]{2,1,0:T(8,128)(2,1)}, bf16[32,128,128]{2,1,0:T(8,128)(2,1)S(1)}, u32[]{:S(2)}, u32[]{:S(2)}) collective-permute-start(bf16[32,128,128]{2,1,0:T(8,128)(2,1)} %bitcast.11), channel_id=1, source_target_pairs={{0,2},{1,3},{2,0},{3,1},{4,6},{5,7},{6,4},{7,5},{8,10},{9,11},{10,... | collective-permute-start | bytes 3145736 | tf_op jit(solution)/shard_map/ppermute | solution.py:148
  5.0 4.8 %collective-permute-start.3 = (bf16[1,128,128]{2,1,0:T(8,128)(2,1)S(1)}, bf16[1,128,128]{2,1,0:T(8,128)(2,1)S(1)}, u32[]{:S(2)}, u32[]{:S(2)}) collective-permute-start(bf16[1,128,128]{2,1,0:T(8,128)(2,1)S(1)} %get-tuple-element.17), channel_id=1, source_target_pairs={{0,16},{1,17},{2,18},{3,19},{4,20},{5,21},{6,22},{7,23},{8,24},{9,... | collective-permute-start | bytes 98312 | tf_op jit(solution)/shard_map/ppermute | solution.py:142
  9.9 4.3 %collective-permute-start.4 = (bf16[2,128,128]{2,1,0:T(8,128)(2,1)S(1)}, bf16[2,128,128]{2,1,0:T(8,128)(2,1)S(1)}, u32[]{:S(2)}, u32[]{:S(2)}) collective-permute-start(bf16[2,128,128]{2,1,0:T(8,128)(2,1)S(1)} %pad_maximum_fusion.3), channel_id=1, source_target_pairs={{0,8},{1,9},{2,10},{3,11},{4,12},{5,13},{6,14},{7,15},{8,0},{9,1},... | collective-permute-start | bytes 196616 | tf_op jit(solution)/shard_map/ppermute | solution.py:142
  14.2 5.0 %collective-permute-start.5 = (bf16[4,128,128]{2,1,0:T(8,128)(2,1)S(1)}, bf16[4,128,128]{2,1,0:T(8,128)(2,1)S(1)}, u32[]{:S(2)}, u32[]{:S(2)}) collective-permute-start(bf16[4,128,128]{2,1,0:T(8,128)(2,1)S(1)} %pad_maximum_fusion.2), channel_id=1, source_target_pairs={{0,4},{1,5},{2,6},{3,7},{4,0},{5,1},{6,2},{7,3},{8,12},{9,13},{10,... | collective-permute-start | bytes 393224 | tf_op jit(solution)/shard_map/ppermute | solution.py:142
  15.8 20.4 %collective-permute-start = (bf16[32,128,128]{2,1,0:T(8,128)(2,1)}, bf16[32,128,128]{2,1,0:T(8,128)(2,1)S(1)}, u32[]{:S(2)}, u32[]{:S(2)}) collective-permute-start(bf16[32,128,128]{2,1,0:T(8,128)(2,1)} %bitcast.12), channel_id=1, source_target_pairs={{0,1},{1,0},{2,3},{3,2},{4,5},{5,4},{6,7},{7,6},{8,9},{9,8},{10,11... | collective-permute-start | bytes 3145736 | tf_op jit(solution)/shard_map/ppermute | solution.py:147
  19.3 12.7 %collective-permute-start.6 = (bf16[8,128,128]{2,1,0:T(8,128)(2,1)S(1)}, bf16[8,128,128]{2,1,0:T(8,128)(2,1)S(1)}, u32[]{:S(2)}, u32[]{:S(2)}) collective-permute-start(bf16[8,128,128]{2,1,0:T(8,128)(2,1)S(1)} %pad_maximum_fusion.1), channel_id=1, source_target_pairs={{0,2},{1,3},{2,0},{3,1},{4,6},{5,7},{6,4},{7,5},{8,10},{9,11},{10,... | collective-permute-start | bytes 786440 | tf_op jit(solution)/shard_map/ppermute | solution.py:142
  27.2 9.0 %collective-permute-start.2 = (bf16[32,128,128]{2,1,0:T(8,128)(2,1)S(1)}, bf16[32,128,128]{2,1,0:T(8,128)(2,1)}, u32[]{:S(2)}, u32[]{:S(2)}) collective-permute-start(bf16[32,128,128]{2,1,0:T(8,128)(2,1)S(1)} %collective-permute-done.1.rest_2_), channel_id=1, source_target_pairs={{0,1},{1,0},{2,3},{3,2},{4,5},{5,4},{6,7},{7,6},{8,9},{9,8},{10,11... | collective-permute-start | bytes 3145736 | tf_op jit(solution)/shard_map/ppermute | solution.py:149
  32.8 2.3 %collective-permute-start.7 = (bf16[16,128,128]{2,1,0:T(8,128)(2,1)}, bf16[16,128,128]{2,1,0:T(8,128)(2,1)}, u32[]{:S(2)}, u32[]{:S(2)}) collective-permute-start(bf16[16,128,128]{2,1,0:T(8,128)(2,1)} %get-tuple-element.18), channel_id=1, source_target_pairs={{0,1},{1,0},{2,3},{3,2},{4,5},{5,4},{6,7},{7,6},{8,9},{9,8},{10,11... | collective-permute-start | bytes 1572872 | tf_op jit(solution)/shard_map/ppermute | solution.py:142
  36.2 1.2 %copy-start = (bf16[4096,128]{1,0:T(8,128)(2,1)S(1)}, bf16[4096,128]{1,0:T(8,128)(2,1)}, u32[]{:S(2)}) copy-start(bf16[4096,128]{1,0:T(8,128)(2,1)} %xc_ref.1) | copy-start | bytes 3145732
  37.4 0.9 copy-start.1
  38.4 0.8 copy-start.2
  39.2 0.8 copy-start.3
  40.0 0.7 copy-start.4
  40.7 0.7 copy-start.5
  41.4 0.7 copy-start.6
  42.1 0.7 copy-start.7
where the time goes:
time: 110 us
  Pallas kernels  67.2 us (61%)
  waiting for transfers between devices  19.8 us (18%)
  local copies, waits for them, and re-layouts  11.8 us (11%)
  starting transfers between devices  9.31 us (8%)
  other arithmetic  1.11 us (1%)
    pallas_call x1, Pallas kernels, on_device(): pl.pallas_call(kernel, grid_spec=grid_spec, out_shape=jax.ShapeDtypeStruc...  67.2 us
    ppermute x5, waiting for transfers between devices, on_device(): lax.ppermute(halo_blocks, ('dom', 'grp'), [(i, i ^ mask) for i in range(n...  12.4 us
    unnamed x21, local copies, waits for them, and re-layouts  9.89 us
    ppermute x1, waiting for transfers between devices, on_device(): far = lax.ppermute(own_blocks, 'grp', [(i, i ^ 2) for i in range(4)])  7.41 us
    ppermute x5, starting transfers between devices, on_device(): lax.ppermute(halo_blocks, ('dom', 'grp'), [(i, i ^ mask) for i in range(n...  6.31 us
    ppermute x1, starting transfers between devices, on_device(): far = lax.ppermute(own_blocks, 'grp', [(i, i ^ 2) for i in range(4)])  3 us
  transfers between devices with their start and end apart: 8, of which 6 were waited for; matrix products, arithmetic and copies ran while one was open for 6% of the time, Pallas kernels for 0%

commit v1 on v0

--- a/solution.py
+++ b/solution.py
@@ -1,7 +1,4 @@
 import functools
-
-import ml_dtypes
-import numpy as np
 
 import jax
 import jax.numpy as jnp
@@ -13,28 +10,11 @@
 CHUNK = 8
 
 
-def _expand_matrix(tile):
-    rows = np.arange(tile)[:, None]
-    cols = np.arange(8 * tile)[None, :]
-    s = cols // tile
-    j = cols % tile
-    hit = rows == (tile // 8) * s + j // 8
-    scale = (2.0 ** (7 - j % 8)).astype(np.float32)
-    return np.where(hit, scale, 0.0).astype(ml_dtypes.bfloat16)
-
-
-def _perm_matrix(tile):
-    kk = tile // 8
-    rows = np.arange(tile)[:, None]
-    cols = np.arange(tile)[None, :]
-    return rows == 8 * (cols % kk) + cols // kk
-
-
-def _layer_kernel(cols_ref, counts_ref, grp_ref, adj_ref, xc_ref, deg_ref, w_ref, b_ref,
-                  mexp_ref, perm_ref, pick_ref, *rest, per_tile, tile, n_table, n_grp, dev_blocks,
+def _layer_kernel(cols_ref, counts_ref, grp_ref, adj_ref, xc_ref, deg_ref, ws_ref, wn_ref, b_ref,
+                  *rest, per_tile, tile, n_table, n_grp, dev_blocks,
                   levels, per_dev):
     pieces = rest[:n_grp + 1]
-    out_ref, table_ref, sems, words_ref, acc_ref = rest[n_grp + 1:]
+    out_ref, table_ref, sems, words_ref, acc_ref, mexp_ref, perm_ref, pick_ref = rest[n_grp + 1:]
     r = pl.program_id(0)
     count = counts_ref[r]
     g = grp_ref[0]
@@ -43,6 +23,17 @@
 
     @pl.when(r == 0)
     def _():
+        rows = lax.broadcasted_iota(jnp.int32, (tile, 8 * tile), 0)
+        cols = lax.broadcasted_iota(jnp.int32, (tile, 8 * tile), 1)
+        jj = cols % tile
+        hit = rows == (tile // 8) * (cols // tile) + jj // 8
+        scale = lax.shift_left(jnp.ones_like(jj), 7 - jj % 8).astype(jnp.float32)
+        mexp_ref[...] = jnp.where(hit, scale, 0.0).astype(jnp.bfloat16)
+        ri = lax.broadcasted_iota(jnp.int32, (tile, tile), 0)
+        ci = lax.broadcasted_iota(jnp.int32, (tile, tile), 1)
+        kq = tile // 8
+        perm_ref[...] = (ri == 8 * (ci % kq) + ci // kq).astype(jnp.bfloat16)
+        pick_ref[...] = (ci == 8 * (ri % kq) + ri // kq).astype(jnp.float32)
         copies = []
         for d in range(n_grp):
             copies.append(pltpu.make_async_copy(
@@ -106,8 +97,8 @@
     deg_perm = jnp.sum(pick_ref[...] * deg_row, axis=1, keepdims=True)
     avg_perm = (totals / deg_perm).astype(jnp.bfloat16)
     avg = jnp.dot(perm_ref[...], avg_perm, preferred_element_type=jnp.float32).astype(jnp.bfloat16)
-    lhs = jnp.concatenate([xc_ref[...], avg], axis=1)
-    summed = jnp.dot(lhs, w_ref[...], preferred_element_type=jnp.float32) + b_ref[...]
+    summed = (jnp.dot(xc_ref[...], ws_ref[...], preferred_element_type=jnp.float32)
+              + jnp.dot(avg, wn_ref[...], preferred_element_type=jnp.float32) + b_ref[...])
     out_ref[...] = jnp.maximum(summed, 0.0).astype(out_ref.dtype)
 
 
@@ -156,12 +147,7 @@
     grp_idx = jnp.stack([lax.axis_index("grp"), me]).astype(jnp.int32)
 
     deg = degree.reshape(row_blocks, tile_rows)
-    w_cat = jnp.concatenate([w_self, w_neigh], axis=0)
     b2 = bias.reshape(1, hidden)
-    mexp = jnp.asarray(_expand_matrix(tile_rows))
-    perm_np = _perm_matrix(tile_rows)
-    perm = jnp.asarray(perm_np.astype(ml_dtypes.bfloat16))
-    pick = jnp.asarray(perm_np.T.astype(np.float32))
 
     kernel = functools.partial(_layer_kernel, per_tile=per_tile, tile=tile_rows, n_table=n_table,
                                n_grp=n_grp, dev_blocks=row_blocks, levels=levels,
@@ -173,17 +159,18 @@
             pl.BlockSpec((1, per_tile, tile_rows * kk), lambda r, *_: (r, 0, 0)),
             pl.BlockSpec((tile_rows, width), lambda r, *_: (r, 0)),
             pl.BlockSpec((row_blocks, tile_rows), lambda r, *_: (0, 0)),
-            pl.BlockSpec((2 * width, hidden), lambda r, *_: (0, 0)),
+            pl.BlockSpec((width, hidden), lambda r, *_: (0, 0)),
+            pl.BlockSpec((width, hidden), lambda r, *_: (0, 0)),
             pl.BlockSpec((1, hidden), lambda r, *_: (0, 0)),
-            pl.BlockSpec((tile_rows, 8 * tile_rows), lambda r, *_: (0, 0)),
-            pl.BlockSpec((tile_rows, tile_rows), lambda r, *_: (0, 0)),
-            pl.BlockSpec((tile_rows, tile_rows), lambda r, *_: (0, 0)),
         ] + [pl.BlockSpec(memory_space=pl.ANY)] * (n_grp + 1),
         out_specs=pl.BlockSpec((tile_rows, hidden), lambda r, *_: (r, 0)),
         scratch_shapes=[pltpu.VMEM((n_table, tile_rows, width), jnp.bfloat16),
                         pltpu.SemaphoreType.DMA((n_grp + 1,)),
                         pltpu.VMEM((per_tile * kk, tile_rows), jnp.int32),
-                        pltpu.VMEM((tile_rows, width), jnp.float32)],
+                        pltpu.VMEM((tile_rows, width), jnp.float32),
+                        pltpu.VMEM((tile_rows, 8 * tile_rows), jnp.bfloat16),
+                        pltpu.VMEM((tile_rows, tile_rows), jnp.bfloat16),
+                        pltpu.VMEM((tile_rows, tile_rows), jnp.float32)],
     )
     return pl.pallas_call(
         kernel,
@@ -191,7 +178,7 @@
         out_shape=jax.ShapeDtypeStruct((node_rows, hidden), jnp.bfloat16),
         compiler_params=pltpu.CompilerParams(
             dimension_semantics=("arbitrary",), vmem_limit_bytes=48 * 1024 * 1024),
-    )(tile_columns, tile_count, grp_idx, adjacency, x_current, deg, w_cat, b2, mexp, perm, pick, *pieces)
+    )(tile_columns, tile_count, grp_idx, adjacency, x_current, deg, w_self, w_neigh, b2, *pieces)
 
 
 def solution(mesh):

time: 110 us -> 112 us (1.018)
  the two profiles are of different devices: /device:TPU:0 before, /device:TPU:16 now
where the time goes in v1:
time: 112 us
  Pallas kernels  71.2 us (64%)
  waiting for transfers between devices  23 us (21%)
  local copies, waits for them, and re-layouts  11.1 us (10%)
  starting transfers between devices  5.85 us (5%)
    pallas_call x1, Pallas kernels, on_device(): pl.pallas_call(kernel, grid_spec=grid_spec, out_shape=jax.ShapeDtypeStruc...  71.2 us
    ppermute x5, waiting for transfers between devices, on_device(): lax.ppermute(halo_blocks, ('dom', 'grp'), [(i, i ^ mask) for i in range(n...  15.1 us
    unnamed x19, local copies, waits for them, and re-layouts  9.15 us
    ppermute x1, waiting for transfers between devices, on_device(): far = lax.ppermute(own_blocks, 'grp', [(i, i ^ 2) for i in range(4)])  7.84 us
    ppermute x5, starting transfers between devices, on_device(): lax.ppermute(halo_blocks, ('dom', 'grp'), [(i, i ^ mask) for i in range(n...  4.32 us
  transfers between devices with their start and end apart: 8, of which 6 were waited for; matrix products, arithmetic and copies ran while one was open for 5% of the time, Pallas kernels for 0%

profile of v1, /device:TPU:16, one launch (start us, length us, event | category | flops | bytes accessed | tf_op | source)
XLA Modules:
  0.0 112.0 jit_solution(3521034550417500157)
XLA Ops:
  0.0 1.5 %collective-permute-start.1 = (bf16[32,128,128]{2,1,0:T(8,128)(2,1)}, bf16[32,128,128]{2,1,0:T(8,128)(2,1)S(1)}, u32[]{:S(2)}, u32[]{:S(2)}) collective-permute-start(bf16[32,128,128]{2,1,0:T(8,128)(2,1)} %bitcast.11), channel_id=1, source_target_pairs={{0,2},{1,3},{2,0},{3,1},{4,6},{5,7},{6,4},{7,5},{8,10},{9,11},{10,... | collective-permute-start | bytes 3145736 | tf_op jit(solution)/shard_map/ppermute | solution.py:139
  2.2 1.4 %constant_dynamic-update-slice_fusion.4 = (bf16[16,128,128]{2,1,0:T(8,128)(2,1)}, bf16[1,128,128]{2,1,0:T(8,128)(2,1)S(1)}) fusion(bf16[32,128,128]{2,1,0:T(8,128)(2,1)} %bitcast.16, s32[]{:T(128)} %bitcast.7), kind=kLoop, calls=%fused_computation.7 | loop fusion | bytes 98308
  3.6 0.3 collective-permute-start.3
  3.9 4.5 %collective-permute-done.3 = bf16[1,128,128]{2,1,0:T(8,128)(2,1)S(1)} collective-permute-done((bf16[1,128,128]{2,1,0:T(8,128)(2,1)S(1)}, bf16[1,128,128]{2,1,0:T(8,128)(2,1)S(1)}, u32[]{:S(2)}, u32[]{:S(2)}) %collective-permute-start.3) | collective-permute-done | bytes 32800 | tf_op jit(solution)/shard_map/ppermute | solution.py:133
  8.4 1.9 %collective-permute-start.4 = (bf16[2,128,128]{2,1,0:T(8,128)(2,1)S(1)}, bf16[2,128,128]{2,1,0:T(8,128)(2,1)S(1)}, u32[]{:S(2)}, u32[]{:S(2)}) collective-permute-start(bf16[2,128,128]{2,1,0:T(8,128)(2,1)S(1)} %pad_maximum_fusion.2), channel_id=1, source_target_pairs={{0,8},{1,9},{2,10},{3,11},{4,12},{5,13},{6,14},{7,15},{8,0},{9,1},... | collective-permute-start | bytes 196616 | tf_op jit(solution)/shard_map/ppermute | solution.py:133
  10.3 2.5 %collective-permute-done.4 = bf16[2,128,128]{2,1,0:T(8,128)(2,1)S(1)} collective-permute-done((bf16[2,128,128]{2,1,0:T(8,128)(2,1)S(1)}, bf16[2,128,128]{2,1,0:T(8,128)(2,1)S(1)}, u32[]{:S(2)}, u32[]{:S(2)}) %collective-permute-start.4) | collective-permute-done | bytes 65568 | tf_op jit(solution)/shard_map/ppermute | solution.py:133
  12.8 1.6 %collective-permute-start.5 = (bf16[4,128,128]{2,1,0:T(8,128)(2,1)S(1)}, bf16[4,128,128]{2,1,0:T(8,128)(2,1)S(1)}, u32[]{:S(2)}, u32[]{:S(2)}) collective-permute-start(bf16[4,128,128]{2,1,0:T(8,128)(2,1)S(1)} %pad_maximum_fusion.1), channel_id=1, source_target_pairs={{0,4},{1,5},{2,6},{3,7},{4,0},{5,1},{6,2},{7,3},{8,12},{9,13},{10,... | collective-permute-start | bytes 393224 | tf_op jit(solution)/shard_map/ppermute | solution.py:133
  14.3 0.0 collective-permute-start
  14.3 3.5 %collective-permute-done.5 = bf16[4,128,128]{2,1,0:T(8,128)(2,1)S(1)} collective-permute-done((bf16[4,128,128]{2,1,0:T(8,128)(2,1)S(1)}, bf16[4,128,128]{2,1,0:T(8,128)(2,1)S(1)}, u32[]{:S(2)}, u32[]{:S(2)}) %collective-permute-start.5) | collective-permute-done | bytes 131104 | tf_op jit(solution)/shard_map/ppermute | solution.py:133
  17.8 0.6 collective-permute-start.6
  18.4 7.8 %collective-permute-done.1.rest_2_ = bf16[32,128,128]{2,1,0:T(8,128)(2,1)S(1)} collective-permute-done((bf16[32,128,128]{2,1,0:T(8,128)(2,1)}, bf16[32,128,128]{2,1,0:T(8,128)(2,1)S(1)}, u32[]{:S(2)}, u32[]{:S(2)}) %collective-permute-start.1) | collective-permute-done | bytes 1048608 | tf_op jit(solution)/shard_map/ppermute | solution.py:139
  26.2 0.0 collective-permute-start.2
  26.2 0.6 constant_dynamic-update-slice_fusion.3
  26.9 0.6 constant_dynamic-update-slice_fusion.2
  27.5 0.7 constant_dynamic-update-slice_fusion.1
  28.2 2.5 %collective-permute-done.6 = bf16[8,128,128]{2,1,0:T(8,128)(2,1)S(1)} collective-permute-done((bf16[8,128,128]{2,1,0:T(8,128)(2,1)S(1)}, bf16[8,128,128]{2,1,0:T(8,128)(2,1)S(1)}, u32[]{:S(2)}, u32[]{:S(2)}) %collective-permute-start.6) | collective-permute-done | bytes 262176 | tf_op jit(solution)/shard_map/ppermute | solution.py:133
  30.7 0.8 constant_dynamic-update-slice_fusion
  31.5 0.0 collective-permute-start.7
  31.5 0.1 pad_add_fusion.grp_ref
  31.6 2.2 %collective-permute-done.7 = bf16[16,128,128]{2,1,0:T(8,128)(2,1)} collective-permute-done((bf16[16,128,128]{2,1,0:T(8,128)(2,1)}, bf16[16,128,128]{2,1,0:T(8,128)(2,1)}, u32[]{:S(2)}, u32[]{:S(2)}) %collective-permute-start.7) | collective-permute-done | bytes 524320 | tf_op jit(solution)/shard_map/ppermute | solution.py:133
  33.8 1.1 %constant_dynamic-update-slice_fusion.5.rest_4_ = bf16[32,128,128]{2,1,0:T(8,128)(2,1)S(1)} fusion(bf16[32,128,128]{2,1,0:T(8,128)(2,1)S(1)} %get-tuple-element.19, bf16[16,128,128]{2,1,0:T(8,128)(2,1)} %collective-permute-done.7), kind=kLoop, calls=%fused_computation.8 | loop fusion | bytes 1048576 | tf_op jit(solution)/shard_map/concatenate | solution.py:134
  34.9 0.0 collective-permute-done.rest_1_
  34.9 0.0 collective-permute-done.2.rest_3_
  34.9 0.0 copy-start
  35.0 1.2 %copy-done = bf16[4096,128]{1,0:T(8,128)(2,1)S(1)} copy-done((bf16[4096,128]{1,0:T(8,128)(2,1)S(1)}, bf16[4096,128]{1,0:T(8,128)(2,1)}, u32[]{:S(2)}) %copy-start) | copy-done | bytes 1048600
  36.2 0.0 copy-start.1
  36.2 0.9 copy-done.1
  37.1 0.0 copy-start.2
  37.1 0.9 copy-done.2
  38.0 0.0 copy-start.3
  38.0 0.7 copy-done.3
  38.7 0.0 copy-start.4
  38.7 0.7 copy-done.4
  39.4 0.0 copy-start.5
  39.4 0.7 copy-done.5
  40.1 0.0 copy-start.6
  40.1 0.7 copy-done.6
  40.7 71.2 %shard_map.100 = bf16[4096,512]{1,0:T(8,128)(2,1)} custom-call(s32[32,40]{1,0:T(8,128)S(1)} %copy-done.3, s32[32]{0:T(128)S(1)} %copy-done.6, s32[2]{0:T(128)S(1)} %pad_add_fusion.grp_ref, s32[32,40,2048]{2,1,0:T(8,128)} %adj_ref.1, bf16[4096,128]{1,0:T(8,128)(2,1)S(1)} %copy-done, s32[32,128]{1,0:T(8,128)S(1)} %bitcast.14, bf16[128,512]{1,0:T(8,128)(2,1)S(1)} %copy-done.1, ...), custom_call_target="tpu_custom_call" | custom-call | tf_op jit(solution)/shard_map/pallas_call | solution.py:175
  (4 shorter events, 0.1 us)
Async XLA Ops:
  0.0 26.2 %collective-permute-start.1 = (bf16[32,128,128]{2,1,0:T(8,128)(2,1)}, bf16[32,128,128]{2,1,0:T(8,128)(2,1)S(1)}, u32[]{:S(2)}, u32[]{:S(2)}) collective-permute-start(bf16[32,128,128]{2,1,0:T(8,128)(2,1)} %bitcast.11), channel_id=1, source_target_pairs={{0,2},{1,3},{2,0},{3,1},{4,6},{5,7},{6,4},{7,5},{8,10},{9,11},{10,... | collective-permute-start | bytes 3145736 | tf_op jit(solution)/shard_map/ppermute | solution.py:139
  3.6 4.8 %collective-permute-start.3 = (bf16[1,128,128]{2,1,0:T(8,128)(2,1)S(1)}, bf16[1,128,128]{2,1,0:T(8,128)(2,1)S(1)}, u32[]{:S(2)}, u32[]{:S(2)}) collective-permute-start(bf16[1,128,128]{2,1,0:T(8,128)(2,1)S(1)} %get-tuple-element.17), channel_id=1, source_target_pairs={{0,16},{1,17},{2,18},{3,19},{4,20},{5,21},{6,22},{7,23},{8,24},{9,... | collective-permute-start | bytes 98312 | tf_op jit(solution)/shard_map/ppermute | solution.py:133
  8.4 4.3 %collective-permute-start.4 = (bf16[2,128,128]{2,1,0:T(8,128)(2,1)S(1)}, bf16[2,128,128]{2,1,0:T(8,128)(2,1)S(1)}, u32[]{:S(2)}, u32[]{:S(2)}) collective-permute-start(bf16[2,128,128]{2,1,0:T(8,128)(2,1)S(1)} %pad_maximum_fusion.2), channel_id=1, source_target_pairs={{0,8},{1,9},{2,10},{3,11},{4,12},{5,13},{6,14},{7,15},{8,0},{9,1},... | collective-permute-start | bytes 196616 | tf_op jit(solution)/shard_map/ppermute | solution.py:133
  12.8 5.0 %collective-permute-start.5 = (bf16[4,128,128]{2,1,0:T(8,128)(2,1)S(1)}, bf16[4,128,128]{2,1,0:T(8,128)(2,1)S(1)}, u32[]{:S(2)}, u32[]{:S(2)}) collective-permute-start(bf16[4,128,128]{2,1,0:T(8,128)(2,1)S(1)} %pad_maximum_fusion.1), channel_id=1, source_target_pairs={{0,4},{1,5},{2,6},{3,7},{4,0},{5,1},{6,2},{7,3},{8,12},{9,13},{10,... | collective-permute-start | bytes 393224 | tf_op jit(solution)/shard_map/ppermute | solution.py:133
  14.3 20.6 %collective-permute-start = (bf16[32,128,128]{2,1,0:T(8,128)(2,1)}, bf16[32,128,128]{2,1,0:T(8,128)(2,1)S(1)}, u32[]{:S(2)}, u32[]{:S(2)}) collective-permute-start(bf16[32,128,128]{2,1,0:T(8,128)(2,1)} %bitcast.12), channel_id=1, source_target_pairs={{0,1},{1,0},{2,3},{3,2},{4,5},{5,4},{6,7},{7,6},{8,9},{9,8},{10,11... | collective-permute-start | bytes 3145736 | tf_op jit(solution)/shard_map/ppermute | solution.py:138
  17.8 12.9 %collective-permute-start.6 = (bf16[8,128,128]{2,1,0:T(8,128)(2,1)S(1)}, bf16[8,128,128]{2,1,0:T(8,128)(2,1)S(1)}, u32[]{:S(2)}, u32[]{:S(2)}) collective-permute-start(bf16[8,128,128]{2,1,0:T(8,128)(2,1)S(1)} %pad_maximum_fusion), channel_id=1, source_target_pairs={{0,2},{1,3},{2,0},{3,1},{4,6},{5,7},{6,4},{7,5},{8,10},{9,11},{10,... | collective-permute-start | bytes 786440 | tf_op jit(solution)/shard_map/ppermute | solution.py:133
  26.2 8.7 %collective-permute-start.2 = (bf16[32,128,128]{2,1,0:T(8,128)(2,1)S(1)}, bf16[32,128,128]{2,1,0:T(8,128)(2,1)}, u32[]{:S(2)}, u32[]{:S(2)}) collective-permute-start(bf16[32,128,128]{2,1,0:T(8,128)(2,1)S(1)} %collective-permute-done.1.rest_2_), channel_id=1, source_target_pairs={{0,1},{1,0},{2,3},{3,2},{4,5},{5,4},{6,7},{7,6},{8,9},{9,8},{10,11... | collective-permute-start | bytes 3145736 | tf_op jit(solution)/shard_map/ppermute | solution.py:140
  31.5 2.3 %collective-permute-start.7 = (bf16[16,128,128]{2,1,0:T(8,128)(2,1)}, bf16[16,128,128]{2,1,0:T(8,128)(2,1)}, u32[]{:S(2)}, u32[]{:S(2)}) collective-permute-start(bf16[16,128,128]{2,1,0:T(8,128)(2,1)} %get-tuple-element.18), channel_id=1, source_target_pairs={{0,1},{1,0},{2,3},{3,2},{4,5},{5,4},{6,7},{7,6},{8,9},{9,8},{10,11... | collective-permute-start | bytes 1572872 | tf_op jit(solution)/shard_map/ppermute | solution.py:133
  34.9 1.2 %copy-start = (bf16[4096,128]{1,0:T(8,128)(2,1)S(1)}, bf16[4096,128]{1,0:T(8,128)(2,1)}, u32[]{:S(2)}) copy-start(bf16[4096,128]{1,0:T(8,128)(2,1)} %xc_ref.1) | copy-start | bytes 3145732
  36.2 0.9 copy-start.1
  37.1 0.9 copy-start.2
  38.0 0.7 copy-start.3
  38.7 0.7 copy-start.4
  39.4 0.7 copy-start.5
  40.1 0.7 copy-start.6
